TPU v7x, 32 devices: a whole 2x2x4 slice. The times are simulated.
32 devices in a mesh: region: 2 (over x), east: 8 (over z, y), north: 2 (over core).
Axes of the slice: x: 2, y: 2, z: 4, core: 2. Of those that a mesh axis runs over, the one named last changes fastest.
Arguments:
- photos: bfloat16 [1024, 4, 16384], P(('region', 'east', 'north')), parts along dimension 0, may hold values from -6 to 6
- footprint: int32 [1024, 1], P(('region', 'east', 'north')), parts along dimension 0, may hold values from 0 to 15; in each aligned block of 32 rows (0 to 31, 32 to 63, ...) at most 2 rows name the same one
- placement: int32 [1024], P(('region', 'east', 'north')), parts along dimension 0, may hold values from 0 to 15
- mask_rows: int32 [1024, 2], P(('region', 'east', 'north')), parts along dimension 0, may hold values from 0 to 128, as said below
- tile_scale: bfloat16 [1024], P(('region', 'east', 'north')), parts along dimension 0, may hold values from 0.5 to 2
Outputs:
- band_zero: bfloat16 [4, 2048, 4096], P(None, ('region', 'north'), 'east'), parts along dimension 1
- band_one: bfloat16 [4, 1024, 2048], P(None, ('region', 'north'), 'east'), parts along dimension 1
- band_two: bfloat16 [4, 512, 1024], P(None, ('region', 'north'), 'east'), parts along dimension 1
- band_three: bfloat16 [4, 256, 512], P(None, 'region'), parts along dimension 1
- apex: bfloat16 [4, 128, 256], P(None, 'region'), parts along dimension 1
There are 2 independent parts, one for each index of `region`. A program takes and returns all parts, laid end to end along the dimension named above; each array names one. Nothing has to cross between parts.
Inputs may be any that keep to these rules, and one draw needn't show every extreme that they name: `footprint`: among the 32 rows of one device no tile is named more than 2 times. `mask_rows`: each row holds a first row below one past the last row.
All inputs are finite; a program needn't handle non-finite values.
Results may differ from a plain program's by a relative error of at most 0.001.
Values may be sent and summed in bfloat16 or wider, within the bound.
No kernel may reach another device: no remote copies, remote signals or barrier semaphores. Data moves between devices by JAX's collectives and lax.ppermute only.
A program may use at most 128 MiB of HBM per device.

v0:
```python
import jax
import jax.numpy as jnp
from jax import lax
from jax.sharding import PartitionSpec as P

BANDS = 4
PATCH = 128
TILE = 512
CAP = 2
BLOCKS = 16
KERNEL = (0.0625, 0.25, 0.375, 0.25, 0.0625)
FLOOR = 0.1
MARGINS = (22, 10, 4, 1)


def padded_2(block, sides, width):
    for axis, dim in sides:
        count = lax.axis_size(axis)
        forward = [(i, i + 1) for i in range(count - 1)]
        backward = [(target, source) for source, target in forward]
        low = lax.ppermute(
            lax.slice_in_dim(block, block.shape[dim] - width, None, axis=dim), axis, forward
        )
        high = lax.ppermute(lax.slice_in_dim(block, 0, width, axis=dim), axis, backward)
        block = jnp.concatenate([low, block, high], axis=dim)
    return block


def tap_table(offset, scale):
    table = jnp.zeros(offset.shape, jnp.float32)
    for tap_index in range(5):
        table = table + jnp.where(offset == tap_index, scale * KERNEL[tap_index], 0.0)
    return table


def reduce_table(size_in):
    size_out = (size_in - 3) // 2
    out_index = jnp.arange(size_out, dtype=jnp.int32)
    in_index = jnp.arange(size_in, dtype=jnp.int32)
    return tap_table(in_index[None, :] - 2 * out_index[:, None], 1.0)


def expand_table(size_in):
    size_out = 2 * (size_in - 2)
    out_index = jnp.arange(size_out, dtype=jnp.int32)
    in_index = jnp.arange(size_in, dtype=jnp.int32)
    return tap_table(2 * in_index[None, :] - out_index[:, None], 2.0)


def apply_tables(padded, row_table, col_table):
    rows_done = jnp.einsum(
        "ih,chw->ciw",
        row_table,
        padded,
        precision=lax.Precision.HIGHEST,
        preferred_element_type=jnp.float32,
    )
    return jnp.einsum(
        "ciw,jw->cij",
        rows_done,
        col_table,
        precision=lax.Precision.HIGHEST,
        preferred_element_type=jnp.float32,
    )


def reduce_padded(padded):
    return apply_tables(padded, reduce_table(padded.shape[1]), reduce_table(padded.shape[2]))


def expand_padded(padded):
    return apply_tables(padded, expand_table(padded.shape[1]), expand_table(padded.shape[2]))


def normalize(grid_field):
    return grid_field[:-1] / jnp.maximum(grid_field[-1:], FLOOR)


def crop_margin(grid_field, margin, keep):
    cut = margin - keep
    return grid_field[:, cut : grid_field.shape[1] - cut, cut : grid_field.shape[2] - cut]


def mask_region(grid_field, margin, tile_side, north_pos, east_pos, north_count, east_count):
    row_global = north_pos * tile_side + jnp.arange(grid_field.shape[1], dtype=jnp.int32) - margin
    col_global = east_pos * tile_side + jnp.arange(grid_field.shape[2], dtype=jnp.int32) - margin
    row_keep = (row_global >= 0) & (row_global < north_count * tile_side)
    col_keep = (col_global >= 0) & (col_global < east_count * tile_side)
    keep_table = (row_keep[:, None] & col_keep[None, :]).astype(jnp.float32)
    return grid_field * keep_table[None, :, :]


def body(photos, footprint, placement, mask_rows, tile_scale):
    east_count = lax.axis_size("east")
    north_count = lax.axis_size("north")
    owners = east_count * north_count
    photo_count = photos.shape[0]
    slot_total = owners * CAP
    target = footprint[:, 0]
    member_table = (target[:, None] == jnp.arange(owners, dtype=jnp.int32)[None, :]).astype(
        jnp.int32
    )
    earlier_count = jnp.cumsum(member_table, axis=0) - member_table
    place_rank = jnp.sum(earlier_count * member_table, axis=1)
    slot_index = target * CAP + place_rank
    slot_match = slot_index[None, :] == jnp.arange(slot_total, dtype=jnp.int32)[:, None]
    filled = jnp.any(slot_match, axis=1)
    source = jnp.sum(
        jnp.where(slot_match, jnp.arange(photo_count, dtype=jnp.int32)[None, :], 0), axis=1
    )
    record = jnp.stack(
        [
            tile_scale.astype(jnp.float32),
            placement.astype(jnp.float32),
            mask_rows[:, 0].astype(jnp.float32),
            mask_rows[:, 1].astype(jnp.float32),
            jnp.ones((photo_count,), jnp.float32),
        ],
        axis=1,
    ).astype(jnp.bfloat16)
    send_photos = jnp.where(filled[:, None, None], photos[source], jnp.zeros((), jnp.bfloat16))
    send_record = jnp.where(filled[:, None], record[source], jnp.zeros((), jnp.bfloat16))
    got_photos, got_record = (
        lax.all_to_all(send_photos, ("east", "north"), split_axis=0, concat_axis=0, tiled=True),
        lax.all_to_all(send_record, ("east", "north"), split_axis=0, concat_axis=0, tiled=True),
    )
    record_value = got_record.astype(jnp.float32)
    gain_scale = record_value[:, 0]
    block_index = record_value[:, 1].astype(jnp.int32)
    lower_row = record_value[:, 2:3]
    upper_row = record_value[:, 3:4]
    live_flag = record_value[:, 4]
    side_index = jnp.arange(PATCH, dtype=jnp.int32)
    edge_weight = (1 + jnp.minimum(side_index, PATCH - 1 - side_index)).astype(jnp.float32)
    feather = edge_weight[:, None] * edge_weight[None, :] / float((PATCH // 2) ** 2)
    side_float = side_index.astype(jnp.float32)
    inside = ((side_float[None, :] >= lower_row) & (side_float[None, :] < upper_row)).astype(
        jnp.float32
    ) * live_flag[:, None]
    weight = inside[:, :, None] * feather[None, :, :]
    gain_value = gain_scale[:, None, None] * weight
    window_photos = got_photos.reshape(slot_total, BANDS, PATCH, PATCH)
    weighted = window_photos.astype(jnp.float32) * gain_value[:, None, :, :]
    block_match = (block_index[None, :] == jnp.arange(BLOCKS, dtype=jnp.int32)[:, None]).astype(
        jnp.float32
    )
    band_sums = jnp.einsum(
        "bk,kcrs->bcrs",
        block_match,
        weighted,
        precision=lax.Precision.HIGHEST,
        preferred_element_type=jnp.float32,
    )
    weight_sums = jnp.einsum(
        "bk,krs->brs",
        block_match,
        weight,
        precision=lax.Precision.HIGHEST,
        preferred_element_type=jnp.float32,
    )
    summed = jnp.concatenate([band_sums, weight_sums[:, None]], axis=1)
    side_blocks = TILE // PATCH
    strips = []
    for block_row in range(side_blocks):
        strips.append(
            jnp.concatenate(
                [summed[block_row * side_blocks + block_col] for block_col in range(side_blocks)],
                axis=2,
            )
        )
    canvas = jnp.concatenate(strips, axis=1)
    results = []
    east_pos = lax.axis_index("east")
    north_pos = lax.axis_index("north")
    grown = padded_2(canvas, (("east", 2), ("north", 1)), MARGINS[0])
    for depth_step in range(3):
        margin_now = MARGINS[depth_step]
        margin_next = MARGINS[depth_step + 1]
        coarse = reduce_padded(grown)
        coarse = mask_region(
            coarse,
            margin_next,
            TILE >> depth_step + 1,
            north_pos,
            east_pos,
            north_count,
            east_count,
        )
        own_field = crop_margin(grown, margin_now, 0)
        coarse_normal = normalize(crop_margin(coarse, margin_next, 1))
        laplace_band = normalize(own_field) - expand_padded(coarse_normal)
        results.append(laplace_band.astype(jnp.bfloat16))
        grown = coarse
    level_field = crop_margin(grown, MARGINS[3], 0)
    stacked = lax.all_gather(level_field[None], ("east", "north"), axis=0, tiled=True)
    chan_count, tall_size, wide_size = level_field.shape
    whole_field = stacked.reshape(east_count, north_count, chan_count, tall_size, wide_size)
    whole_field = whole_field.transpose(2, 1, 3, 0, 4).reshape(
        chan_count, north_count * tall_size, east_count * wide_size
    )
    top_field = reduce_padded(jnp.pad(whole_field, ((0, 0), (2, 2), (2, 2))))
    top_normal = normalize(top_field)
    band_three = (
        normalize(whole_field) - expand_padded(jnp.pad(top_normal, ((0, 0), (1, 1), (1, 1))))
    ).astype(jnp.bfloat16)
    apex = top_normal.astype(jnp.bfloat16)
    return (results[0], results[1], results[2], band_three, apex)


def solution(mesh):
    return jax.shard_map(
        body,
        mesh=mesh,
        in_specs=(
            P(("region", "east", "north"), None, None),
            P(("region", "east", "north"), None),
            P(("region", "east", "north")),
            P(("region", "east", "north"), None),
            P(("region", "east", "north")),
        ),
        out_specs=(
            P(None, ("region", "north"), "east"),
            P(None, ("region", "north"), "east"),
            P(None, ("region", "north"), "east"),
            P(None, "region", None),
            P(None, "region", None),
        ),
        check_vma=False,
    )
```

profile of v0, /device:TPU:0, one launch (start us, length us, event | category | flops | bytes accessed | tf_op | source)
XLA Modules:
  0.0 301.0 jit_solution(17203847547347885743)
XLA Ops:
  7.2 0.7 fusion.202
  7.9 0.8 select_reduce_fusion.1
  8.8 0.7 multiply_add_fusion
  9.7 0.8 convert_convert_fusion
  10.5 0.7 convert_bitcast_fusion
  11.1 0.7 stack.16
  12.0 0.6 gather_fusion
  12.6 0.7 broadcast_select_fusion.1
  13.3 7.4 %all-to-all-start = ((bf16[16,2,5]{2,1,0:T(2,128)(2,1)}), bf16[16,2,5]{2,1,0:T(2,128)(2,1)S(1)}, u32[]{:S(2)}, u32[]{:S(2)}) async-start(bf16[16,2,5]{2,1,0:T(2,128)(2,1)} %broadcast_select_fusion.1), calls=%async_computation | async-start | bytes 16384 | tf_op jit(solution)/shard_map/all_to_all | solution.py:125
  20.7 8.0 %gather_fusion.1 = bf16[32,4,16384]{2,1,0:T(4,128)(2,1)} fusion(bf16[32,4,16384]{2,1,0:T(4,128)(2,1)} %param.5, s32[1024]{0:T(1024)S(1)} %pad_clamp_fusion), kind=kCustom, calls=%fused_computation.1 | custom fusion | bytes 8388736 | tf_op jit(solution)/shard_map/gather | solution.py:121
  28.7 5.9 %broadcast_select_fusion = bf16[32,4,16384]{2,1,0:T(4,128)(2,1)} fusion(bf16[32,4,16384]{2,1,0:T(4,128)(2,1)} %gather_fusion.1, pred[32]{0:T(512)(128)(4,1)S(1)} %fusion.201), kind=kLoop, calls=%fused_computation.80 | loop fusion | flops 2097152 | bytes 8388640 | tf_op jit(solution)/shard_map/jit(_where)/select_n | solution.py:121
  34.6 6.1 %all-to-all-start.1 = ((bf16[32,4,16384]{2,1,0:T(4,128)(2,1)}), bf16[32,4,16384]{2,1,0:T(4,128)(2,1)}, u32[]{:S(2)}, u32[]{:S(2)}) async-start(bf16[32,4,16384]{2,1,0:T(4,128)(2,1)} %broadcast_select_fusion), calls=%async_computation.1 | async-start | bytes 8388608 | tf_op jit(solution)/shard_map/all_to_all | solution.py:124
  40.7 0.3 all-gather.3.cloned.1.call-start
  41.2 0.9 and_convert_fusion
  42.1 0.2 fusion.200
  42.3 0.2 slice_reduce_fusion.3
  42.6 2.1 fusion.58
  44.7 0.6 multiply_multiply_fusion
  45.3 73.0 %all-to-all-done.1 = bf16[32,4,16384]{2,1,0:T(4,128)(2,1)} async-done(((bf16[32,4,16384]{2,1,0:T(4,128)(2,1)}), bf16[32,4,16384]{2,1,0:T(4,128)(2,1)}, u32[]{:S(2)}, u32[]{:S(2)}) %all-to-all-start.1) | async-done | bytes 4194336 | tf_op jit(solution)/shard_map/all_to_all | solution.py:124
  118.3 8.9 %reshape.371 = f32[32,4,128,128]{3,2,1,0:T(8,128)} reshape(bf16[32,4,16384]{2,1,0:T(4,128)(2,1)} %all-to-all-done.1) | data formatting | bytes 12582912 | tf_op jit(solution)/shard_map/convert_element_type | solution.py:143
  127.3 10.9 %fusion = f32[16,4,128,128]{3,0,2,1:T(8,128)S(1)} fusion(f32[32,4,128,128]{3,2,1,0:T(8,128)} %reshape.371, f32[32,128,128]{2,0,1:T(8,128)S(1)} %multiply_multiply_fusion, s32[32]{0:T(128)S(1)} %fusion.200), kind=kOutput, calls=%fused_computation.18 | convolution fusion | flops 404750848 | bytes 14680192 | tf_op jit(solution)/shard_map/bk,kcrs->bcrs/dot_general | solution.py:147
  138.2 2.8 fusion.110
  140.9 2.7 fusion.119
  143.8 1.7 maximum_maximum_fusion.2
  145.4 1.1 maximum_maximum_fusion.1
  146.6 2.4 copy.121
  149.0 8.8 %collective-permute-start = (f32[5,512,22]{1,2,0:T(8,128)}, f32[5,512,22]{1,2,0:T(8,128)}, u32[]{:S(2)}, u32[]{:S(2)}) collective-permute-start(f32[5,512,22]{1,2,0:T(8,128)} %copy.121), channel_id=1, source_target_pairs={{0,2},{2,4},{4,6},{6,8},{8,10},{10,12},{12,14},{1,3},{3,5},{5,7},{... | collective-permute-start | bytes 675848 | tf_op jit(solution)/shard_map/ppermute | solution.py:21
  157.8 2.4 copy.122
  160.2 1.3 collective-permute-start.1
  161.6 2.0 collective-permute-done
  163.5 2.5 copy.123
  166.0 11.5 %collective-permute-done.1 = f32[5,512,22]{1,2,0:T(8,128)} collective-permute-done((f32[5,512,22]{1,2,0:T(8,128)}, f32[5,512,22]{1,2,0:T(8,128)}, u32[]{:S(2)}, u32[]{:S(2)}) %collective-permute-start.1) | collective-permute-done | bytes 225312 | tf_op jit(solution)/shard_map/ppermute | solution.py:24
  177.5 2.4 copy.124
  179.9 12.6 %pad_maximum_fusion = f32[5,512,556]{2,1,0:T(8,128)S(1)} fusion(f32[5,512,22]{2,1,0:T(8,128)} %copy.124, f32[5,128,128]{2,1,0:T(8,128)} %bitcast.251, f32[5,128,128]{2,1,0:T(8,128)} %bitcast.257, f32[5,128,128]{2,1,0:T(8,128)} %bitcast.245, f32[5,128,128]{2,1,0:T(8,128)} %bitcast.239, f32[5,128,128]{2,1,0:T(8,128)} %bitcast.233, ...), kind=kLoop, calls=%fused_computation.74 | loop fusion | flops 24197120 | bytes 11386880 | tf_op jit(solution)/shard_map/concatenate | solution.py:25
  192.7 1.3 collective-permute-start.2
  194.0 1.3 collective-permute-start.3
  195.3 3.5 %maximum_maximum_fusion = f32[5,512,512]{2,1,0:T(8,128)} fusion(f32[5,128,128]{2,1,0:T(8,128)S(1)} %bitcast.252, f32[5,128,128]{2,1,0:T(8,128)S(1)} %bitcast.258, f32[5,128,128]{2,1,0:T(8,128)S(1)} %bitcast.246, f32[5,128,128]{2,1,0:T(8,128)S(1)} %bitcast.240, f32[5,128,128]{2,1,0:T(8,128)S(1)} %bitcast.234, f32[5,128,128]{2,1,0:T(8,128)S(1)} %bitcast.228, ...), kind=kLoop, calls=%fused_computation.75 | loop fusion | flops 19660800 | bytes 10485760 | tf_op jit(solution)/shard_map/concatenate | solution.py:171
  198.9 1.2 fusion.67
  200.1 0.5 copy-done.14
  200.6 0.4 copy-done.15
  201.0 12.4 %fusion.1 = f32[5,556,276]{1,2,0:T(8,128)S(1)} fusion(f32[5,22,556]{2,1,0:T(8,128)S(1)} %collective-permute-done.3, f32[5,512,22]{2,1,0:T(8,128)S(1)} %copy-done.15, f32[5,128,128]{2,1,0:T(8,128)S(1)} %bitcast.254, f32[5,128,128]{2,1,0:T(8,128)S(1)} %bitcast.260, f32[5,128,128]{2,1,0:T(8,128)S(1)} %bitcast.248, f32[5,128,128]{2,1,0:T(8,128)S(1)} %bitcast.242, ...), kind=kOutput, calls=%fused_computation.34 | convolution fusion | flops 5150962176 | bytes 9252944 | tf_op jit(solution)/shard_map/ih,chw->ciw/dot_general | solution.py:51
  213.4 7.4 %fusion.54 = f32[5,276,276]{2,1,0:T(8,128)S(1)} fusion(f32[5,556,276]{1,2,0:T(8,128)S(1)} %fusion.1, f32[276,276]{1,0:T(8,128)S(1)} %copy-done.17, s32[276]{0:T(512)S(1)} %iota_multiply_fusion.1), kind=kOutput, calls=%fused_computation.91 | convolution fusion | flops 2543913984 | bytes 4898448 | tf_op jit(solution)/shard_map/ciw,jw->cij/dot_general | solution.py:58
  220.8 2.3 convolution_bitcast_fusion
  223.0 1.4 convolution_multiply_fusion
  224.4 1.7 convolution_bitcast_fusion.3
  226.2 1.2 convolution_multiply_fusion.1
  227.4 0.8 slice.254
  228.5 0.4 convolution_bitcast_fusion.4
  229.0 1.3 fusion.66
  230.5 1.6 convolution_bitcast_fusion.1
  232.1 2.9 fusion.64
  235.0 4.5 %fusion.57 = f32[4,258,512]{2,1,0:T(8,128)S(1)} fusion(f32[5,276,276]{2,1,0:T(8,128)S(1)} %fusion.54, f32[258,258]{1,0:T(8,128)S(1)} %fusion.108, s32[258]{0:T(512)S(1)} %iota_multiply_fusion), kind=kOutput, calls=%fused_computation.93 | convolution fusion | flops 1638124544 | bytes 4143104 | tf_op jit(solution)/shard_map/ih,chw->ciw/dot_general | solution.py:51
  239.6 9.1 %fusion.42 = bf16[4,512,512]{2,1,0:T(8,128)(2,1)} fusion(f32[5,512,512]{2,1,0:T(8,128)S(1)} %bitcast.262, f32[512,512]{1,0:T(8,128)S(1)} %copy-done.18, f32[4,258,512]{2,1,0:T(8,128)S(1)} %fusion.57, s32[258]{0:T(512)S(1)} %iota_multiply_fusion), kind=kOutput, calls=%fused_computation.78 | convolution fusion | flops 3251518464 | bytes 9454600 | tf_op jit(solution)/shard_map/ciw,jw->cij/dot_general | solution.py:58
  248.7 26.4 %all-gather.3.cloned.1.call-done = f32[80,64,64]{2,1,0:T(8,128)} async-done(((f32[5,64,64]{2,1,0:T(8,128)}), f32[80,64,64]{2,1,0:T(8,128)}) %all-gather.3.cloned.1.call-update) | async-done | bytes 1310736 | tf_op jit(solution)/shard_map/all_gather | solution.py:195
  275.1 3.4 %copy.153 = f32[8,2,5,64,64]{4,0,3,1,2:T(8,128)S(1)} copy(f32[8,2,5,64,64]{4,3,2,1,0:T(8,128)} %bitcast.263) | data formatting | bytes 2621440 | tf_op jit(solution)/shard_map/reshape | solution.py:197
  278.5 1.7 reshape.369
  280.1 1.5 slice.255
  281.7 0.4 copy-done.16
  282.0 1.6 fusion.61
  283.6 1.2 fusion.86
  284.8 0.7 fusion.363
  285.5 2.2 convolution_bitcast_fusion.2
  287.7 1.5 slice.198
  289.3 4.4 %fusion.65 = bf16[4,128,512]{2,1,0:T(8,128)(2,1)} fusion(f32[4,128,258]{1,2,0:T(8,128)} %convolution_bitcast_fusion.2, f32[4,128,512]{2,1,0:T(8,128)} %slice.198, f32[128,512]{1,0:T(8,128)S(1)} %max.70, s32[258]{0:T(512)S(1)} %iota_multiply_fusion), kind=kOutput, calls=%fused_computation.102 | convolution fusion | flops 814365696 | bytes 2364424 | tf_op jit(solution)/shard_map/ciw,jw->cij/dot_general | solution.py:58
  (78 shorter events, 1.7 us)
Async XLA Ops:
  13.3 21.3 %all-to-all-start = ((bf16[16,2,5]{2,1,0:T(2,128)(2,1)}), bf16[16,2,5]{2,1,0:T(2,128)(2,1)S(1)}, u32[]{:S(2)}, u32[]{:S(2)}) async-start(bf16[16,2,5]{2,1,0:T(2,128)(2,1)} %broadcast_select_fusion.1), calls=%async_computation | async-start | bytes 16384 | tf_op jit(solution)/shard_map/all_to_all | solution.py:125
  34.6 83.7 %all-to-all-start.1 = ((bf16[32,4,16384]{2,1,0:T(4,128)(2,1)}), bf16[32,4,16384]{2,1,0:T(4,128)(2,1)}, u32[]{:S(2)}, u32[]{:S(2)}) async-start(bf16[32,4,16384]{2,1,0:T(4,128)(2,1)} %broadcast_select_fusion), calls=%async_computation.1 | async-start | bytes 8388608 | tf_op jit(solution)/shard_map/all_to_all | solution.py:124
  40.7 234.4 %all-gather.3.cloned.1.call-start = ((), (), s32[]{:S(2)}) async-start(), calls=%async_computation.2 | async-start | bytes 2785280 | tf_op jit(solution)/shard_map/all_gather | solution.py:195
  127.3 10.9 %copy-start.12 = (f32[16,1,128,128]{3,0,2,1:T(8,128)S(1)}, f32[16,1,128,128]{3,0,2,1:T(8,128)}, u32[]{:S(2)}) copy-start(f32[16,1,128,128]{3,0,2,1:T(8,128)} %fusion.58) | copy-start | bytes 3145732
  143.7 1.7 copy-start
  143.7 1.7 copy-start.2
  143.7 1.7 copy-start.4
  143.7 1.7 copy-start.6
  143.7 1.7 copy-start.8
  143.7 1.7 copy-start.10
  149.0 14.5 %collective-permute-start = (f32[5,512,22]{1,2,0:T(8,128)}, f32[5,512,22]{1,2,0:T(8,128)}, u32[]{:S(2)}, u32[]{:S(2)}) collective-permute-start(f32[5,512,22]{1,2,0:T(8,128)} %copy.121), channel_id=1, source_target_pairs={{0,2},{2,4},{4,6},{6,8},{8,10},{10,12},{12,14},{1,3},{3,5},{5,7},{... | collective-permute-start | bytes 675848 | tf_op jit(solution)/shard_map/ppermute | solution.py:21
  160.2 17.3 %collective-permute-start.1 = (f32[5,512,22]{1,2,0:T(8,128)}, f32[5,512,22]{1,2,0:T(8,128)}, u32[]{:S(2)}, u32[]{:S(2)}) collective-permute-start(f32[5,512,22]{1,2,0:T(8,128)} %copy.122), channel_id=1, source_target_pairs={{2,0},{4,2},{6,4},{8,6},{10,8},{12,10},{14,12},{3,1},{5,3},{7,5},{... | collective-permute-start | bytes 675848 | tf_op jit(solution)/shard_map/ppermute | solution.py:24
  179.9 15.4 %copy-start.1 = (f32[1,5,128,128]{3,0,2,1:T(1,128)S(1)}, f32[1,5,128,128]{3,0,2,1:T(1,128)}, u32[]{:S(2)}) copy-start(f32[1,5,128,128]{3,0,2,1:T(1,128)} %copy-done) | copy-start | bytes 983044
  179.9 15.4 %copy-start.3 = (f32[1,5,128,128]{3,0,2,1:T(1,128)S(1)}, f32[1,5,128,128]{3,0,2,1:T(1,128)}, u32[]{:S(2)}) copy-start(f32[1,5,128,128]{3,0,2,1:T(1,128)} %copy-done.2) | copy-start | bytes 983044
  179.9 15.4 %copy-start.5 = (f32[1,5,128,128]{3,0,2,1:T(1,128)S(1)}, f32[1,5,128,128]{3,0,2,1:T(1,128)}, u32[]{:S(2)}) copy-start(f32[1,5,128,128]{3,0,2,1:T(1,128)} %copy-done.4) | copy-start | bytes 983044
  179.9 15.4 %copy-start.7 = (f32[1,5,128,128]{3,0,2,1:T(1,128)S(1)}, f32[1,5,128,128]{3,0,2,1:T(1,128)}, u32[]{:S(2)}) copy-start(f32[1,5,128,128]{3,0,2,1:T(1,128)} %copy-done.6) | copy-start | bytes 983044
  179.9 15.4 %copy-start.9 = (f32[1,5,128,128]{3,0,2,1:T(1,128)S(1)}, f32[1,5,128,128]{3,0,2,1:T(1,128)}, u32[]{:S(2)}) copy-start(f32[1,5,128,128]{3,0,2,1:T(1,128)} %copy-done.8) | copy-start | bytes 983044
  179.9 15.4 %copy-start.11 = (f32[1,5,128,128]{3,0,2,1:T(1,128)S(1)}, f32[1,5,128,128]{3,0,2,1:T(1,128)}, u32[]{:S(2)}) copy-start(f32[1,5,128,128]{3,0,2,1:T(1,128)} %copy-done.10) | copy-start | bytes 983044
  192.7 7.5 %collective-permute-start.2 = (f32[5,22,556]{2,1,0:T(8,128)S(1)}, f32[5,22,556]{2,1,0:T(8,128)S(1)}, u32[]{:S(2)}, u32[]{:S(2)}) collective-permute-start(f32[5,22,556]{2,1,0:T(8,128)S(1)} %get-tuple-element.11), channel_id=1, source_target_pairs={{0,1},{2,3},{4,5},{6,7},{8,9},{10,11},{12,13},{14,15},{16,17},{18,... | collective-permute-start | bytes 733928 | tf_op jit(solution)/shard_map/ppermute | solution.py:21
  194.0 6.1 %collective-permute-start.3 = (f32[5,22,556]{2,1,0:T(8,128)S(1)}, f32[5,22,556]{2,1,0:T(8,128)S(1)}, u32[]{:S(2)}, u32[]{:S(2)}) collective-permute-start(f32[5,22,556]{2,1,0:T(8,128)S(1)} %get-tuple-element.12), channel_id=1, source_target_pairs={{1,0},{3,2},{5,4},{7,6},{9,8},{11,10},{13,12},{15,14},{17,16},{19,... | collective-permute-start | bytes 733928 | tf_op jit(solution)/shard_map/ppermute | solution.py:24
  198.9 1.7 copy-start.14
  198.9 2.1 copy-start.15
  200.1 13.2 %copy-start.17 = (f32[276,276]{1,0:T(8,128)S(1)}, f32[276,276]{1,0:T(8,128)}, u32[]{:S(2)}) copy-start(f32[276,276]{1,0:T(8,128)} %and_convert_fusion) | copy-start | bytes 914116
  232.1 7.4 %slice-start = ((s8[5242880]{0:T(1024)(128)(4,1)}), s8[4194304]{0:T(1024)(128)(4,1)S(1)}, s32[]{:S(2)}) async-start(s8[5242880]{0:T(1024)(128)(4,1)} %bitcast.261), calls=%async_computation.3 | async-start | bytes 8388608
  235.0 4.6 %slice-start.1 = ((s8[5242880]{0:T(1024)(128)(4,1)}), s8[1048576]{0:T(1024)(128)(4,1)S(1)}, s32[]{:S(2)}) async-start(s8[5242880]{0:T(1024)(128)(4,1)} %bitcast.261), calls=%async_computation.4 | async-start | bytes 2097152
  235.0 4.6 %copy-start.18 = (f32[512,512]{1,0:T(8,128)S(1)}, f32[512,512]{1,0:T(8,128)}, u32[]{:S(2)}) copy-start(f32[512,512]{1,0:T(8,128)} %fusion.67) | copy-start | bytes 3145732
  280.1 1.9 copy-start.16
  282.0 5.7 %copy-start.13 = (f32[4,2,64,8,64]{4,3,2,1,0:T(8,128)S(1)}, f32[4,2,64,8,64]{4,3,2,1,0:T(8,128)}, u32[]{:S(2)}) copy-start(f32[4,2,64,8,64]{4,3,2,1,0:T(8,128)} %slice.255) | copy-start | bytes 3145732
Sparse Core Ops, SparseCore 0:
  228.6 46.4 all-gather.2
where the time goes:
time: 306 us; the launch traced here: 301 us
  waiting for transfers between devices  113 us (37%)
  matrix products  68.6 us (22%)
  other arithmetic  39.6 us (13%)
  local copies, waits for them, and re-layouts  38.5 us (13%)
  starting transfers between devices  26.4 us (9%)
  between operations  15 us (5%)
    all_to_all x1, waiting for transfers between devices, body(): lax.all_to_all(send_photos, ('east', 'north'), split_axis=0, concat_axis=...  73 us
    dot_general x8, matrix products, apply_tables(): jnp.einsum('ciw,jw->cij', rows_done, col_table, precision=lax.Precision.H...  28.9 us
    dot_general x8, matrix products, apply_tables(): jnp.einsum('ih,chw->ciw', row_table, padded, precision=lax.Precision.HIGH...  26.7 us
    all_gather x1, waiting for transfers between devices, body(): lax.all_gather(level_field[None], ('east', 'north'), axis=0, tiled=True)  26.4 us
    concatenate x1, other arithmetic, padded_2(): block = jnp.concatenate([low, block, high], axis=dim)  12.6 us
    ppermute x2, waiting for transfers between devices, padded_2(): lax.ppermute(lax.slice_in_dim(block, 0, width, axis=dim), axis, backward)  11.5 us
    dot_general x1, matrix products, body(): jnp.einsum('bk,kcrs->bcrs', block_match, weighted, precision=lax.Precisio...  10.9 us
    ppermute x2, starting transfers between devices, padded_2(): lax.ppermute(lax.slice_in_dim(block, block.shape[dim] - width, None, axis...  10.1 us
  transfers between devices with their start and end apart: 7, of which 4 were waited for; matrix products, arithmetic and copies ran while one was open for 16% of the time, Pallas kernels for 0%

commit v1 on v0

--- a/solution.py
+++ b/solution.py
@@ -1,3 +1,4 @@
+import functools
 import jax
 import jax.numpy as jnp
 from jax import lax
@@ -11,6 +12,33 @@
 KERNEL = (0.0625, 0.25, 0.375, 0.25, 0.0625)
 FLOOR = 0.1
 MARGINS = (22, 10, 4, 1)
+
+
+def _obtain_samples(array_in, shard_axis):
+    out_arr = lax.psum(1, shard_axis)
+    step_out = lax.axis_index(shard_axis)
+    ready, frame_out, now = (out_arr, step_out, array_in.shape[0])
+    column = [dd * ready if at == 0 else dd for at, dd in enumerate(array_in.shape)]
+    row_out = z = array_in
+    m = 1
+    f_next = lax.dynamic_update_slice_in_dim(
+        jnp.zeros(column, array_in.dtype), array_in, frame_out * now, axis=0
+    )
+    while m < ready // 2 + 1:
+        row_out = lax.ppermute(row_out, shard_axis, [(at, (at + 1) % ready) for at in range(ready)])
+        f_next = lax.dynamic_update_slice_in_dim(
+            f_next, row_out, (frame_out - m) % ready * now, axis=0
+        )
+        if 2 * m < ready:
+            z = lax.ppermute(z, shard_axis, [(at, (at - 1) % ready) for at in range(ready)])
+            f_next = lax.dynamic_update_slice_in_dim(
+                f_next, z, (frame_out + m) % ready * now, axis=0
+            )
+        m = m + 1
+    return f_next
+
+
+define_ranges = functools.partial(_obtain_samples, shard_axis=("east", "north"))
 
 
 def padded_2(block, sides, width):
@@ -192,7 +220,7 @@
         results.append(laplace_band.astype(jnp.bfloat16))
         grown = coarse
     level_field = crop_margin(grown, MARGINS[3], 0)
-    stacked = lax.all_gather(level_field[None], ("east", "north"), axis=0, tiled=True)
+    stacked = define_ranges(level_field[None])
     chan_count, tall_size, wide_size = level_field.shape
     whole_field = stacked.reshape(east_count, north_count, chan_count, tall_size, wide_size)
     whole_field = whole_field.transpose(2, 1, 3, 0, 4).reshape(

time: 306 us -> 321 us (1.049)
  starting transfers between devices: 26.4 us -> 58.2 us
  between operations: 15 us -> 1.84 us
  other arithmetic: 39.6 us -> 35.6 us
    ppermute x0 -> x15, starting transfers between devices: none -> 31.6 us  [the longest x7 30.1 us: _obtain_samples(): lax.ppermute(z, shard_axis, [(at, (at - 1) % ready) for at in range(ready)])]
    all_gather x1 -> x0, waiting for transfers between devices: 26.4 us -> none  [body(): lax.all_gather(level_field[None], ('east', 'north'), axis=0, tiled=True)]
    ppermute x0 -> x15, waiting for transfers between devices: none -> 25.4 us  [the longest x8 25.4 us: _obtain_samples(): lax.ppermute(row_out, shard_axis, [(at, (at + 1) % ready) for at in range...]
    reshape x1 -> x0, local copies, waits for them, and re-layouts: 3.38 us -> none  [body(): stacked.reshape(east_count, north_count, chan_count, tall_size, wide_size)]
  transfers between devices with their start and end apart: 7 -> 21, of which waited for: 4 -> 11; matrix products, arithmetic and copies ran while one was open for 16% -> 14% of each run, Pallas kernels for 0% -> 0%
where the time goes in v1:
time: 321 us; the launch traced here: 316 us
  waiting for transfers between devices  113 us (35%)
  matrix products  70.2 us (22%)
  starting transfers between devices  58.2 us (18%)
  local copies, waits for them, and re-layouts  37.3 us (12%)
  other arithmetic  35.6 us (11%)
    all_to_all x1, waiting for transfers between devices, body(): lax.all_to_all(send_photos, ('east', 'north'), split_axis=0, concat_axis=...  73 us
    ppermute x7, starting transfers between devices, _obtain_samples(): lax.ppermute(z, shard_axis, [(at, (at - 1) % ready) for at in range(ready)])  30.1 us
    dot_general x8, matrix products, apply_tables(): jnp.einsum('ciw,jw->cij', rows_done, col_table, precision=lax.Precision.H...  29.1 us
    dot_general x8, matrix products, apply_tables(): jnp.einsum('ih,chw->ciw', row_table, padded, precision=lax.Precision.HIGH...  28.1 us
    ppermute x8, waiting for transfers between devices, _obtain_samples(): lax.ppermute(row_out, shard_axis, [(at, (at + 1) % ready) for at in range...  25.4 us
    ppermute x2, waiting for transfers between devices, padded_2(): lax.ppermute(lax.slice_in_dim(block, 0, width, axis=dim), axis, backward)  12.8 us
    concatenate x1, other arithmetic, padded_2(): block = jnp.concatenate([low, block, high], axis=dim)  12.6 us
    dot_general x1, matrix products, body(): jnp.einsum('bk,kcrs->bcrs', block_match, weighted, precision=lax.Precisio...  10.9 us
  transfers between devices with their start and end apart: 21, of which 11 were waited for; matrix products, arithmetic and copies ran while one was open for 14% of the time, Pallas kernels for 0%

profile of v1, /device:TPU:0, one launch (start us, length us, event | category | flops | bytes accessed | tf_op | source)
XLA Modules:
  0.0 316.2 jit_solution(17073846073351647327)
XLA Ops:
  0.6 0.7 fusion.202
  1.4 0.8 select_reduce_fusion.1
  3.2 0.8 convert_convert_fusion
  6.8 7.4 %all-to-all-start = ((bf16[16,2,5]{2,1,0:T(2,128)(2,1)}), bf16[16,2,5]{2,1,0:T(2,128)(2,1)S(1)}, u32[]{:S(2)}, u32[]{:S(2)}) async-start(bf16[16,2,5]{2,1,0:T(2,128)(2,1)} %broadcast_select_fusion.1), calls=%async_computation | async-start | bytes 16384 | tf_op jit(solution)/shard_map/all_to_all | solution.py:153
  14.2 7.9 %gather_fusion.1 = bf16[32,4,16384]{2,1,0:T(4,128)(2,1)} fusion(bf16[32,4,16384]{2,1,0:T(4,128)(2,1)} %param.5, s32[1024]{0:T(1024)S(1)} %pad_clamp_fusion), kind=kCustom, calls=%fused_computation.1 | custom fusion | bytes 8388736 | tf_op jit(solution)/shard_map/gather | solution.py:149
  22.1 5.9 %broadcast_select_fusion = bf16[32,4,16384]{2,1,0:T(4,128)(2,1)} fusion(bf16[32,4,16384]{2,1,0:T(4,128)(2,1)} %gather_fusion.1, pred[32]{0:T(512)(128)(4,1)S(1)} %fusion.201), kind=kLoop, calls=%fused_computation.80 | loop fusion | flops 2097152 | bytes 8388640 | tf_op jit(solution)/shard_map/jit(_where)/select_n | solution.py:149
  28.0 6.5 %all-to-all-start.1 = ((bf16[32,4,16384]{2,1,0:T(4,128)(2,1)}), bf16[32,4,16384]{2,1,0:T(4,128)(2,1)}, u32[]{:S(2)}, u32[]{:S(2)}) async-start(bf16[32,4,16384]{2,1,0:T(4,128)(2,1)} %broadcast_select_fusion), calls=%async_computation.1 | async-start | bytes 8388608 | tf_op jit(solution)/shard_map/all_to_all | solution.py:152
  35.1 0.9 and_convert_fusion
  36.5 2.1 fusion.58
  39.2 73.0 %all-to-all-done.1 = bf16[32,4,16384]{2,1,0:T(4,128)(2,1)} async-done(((bf16[32,4,16384]{2,1,0:T(4,128)(2,1)}), bf16[32,4,16384]{2,1,0:T(4,128)(2,1)}, u32[]{:S(2)}, u32[]{:S(2)}) %all-to-all-start.1) | async-done | bytes 4194336 | tf_op jit(solution)/shard_map/all_to_all | solution.py:152
  112.2 9.0 %reshape.371 = f32[32,4,128,128]{3,2,1,0:T(8,128)} reshape(bf16[32,4,16384]{2,1,0:T(4,128)(2,1)} %all-to-all-done.1) | data formatting | bytes 12582912 | tf_op jit(solution)/shard_map/convert_element_type | solution.py:171
  121.2 10.9 %fusion = f32[16,4,128,128]{3,0,2,1:T(8,128)S(1)} fusion(f32[32,4,128,128]{3,2,1,0:T(8,128)} %reshape.371, f32[32,128,128]{2,0,1:T(8,128)S(1)} %multiply_multiply_fusion, s32[32]{0:T(128)S(1)} %fusion.200), kind=kOutput, calls=%fused_computation.18 | convolution fusion | flops 404750848 | bytes 14680192 | tf_op jit(solution)/shard_map/bk,kcrs->bcrs/dot_general | solution.py:175
  132.1 2.8 fusion.110
  134.8 2.7 fusion.119
  137.7 1.7 maximum_maximum_fusion.2
  139.3 1.1 maximum_maximum_fusion.1
  140.5 2.4 copy.124
  142.9 8.8 %collective-permute-start = (f32[5,512,22]{1,2,0:T(8,128)}, f32[5,512,22]{1,2,0:T(8,128)}, u32[]{:S(2)}, u32[]{:S(2)}) collective-permute-start(f32[5,512,22]{1,2,0:T(8,128)} %copy.124), channel_id=1, source_target_pairs={{0,2},{2,4},{4,6},{6,8},{8,10},{10,12},{12,14},{1,3},{3,5},{5,7},{... | collective-permute-start | bytes 675848 | tf_op jit(solution)/shard_map/ppermute | solution.py:49
  151.7 2.4 copy.125
  154.1 1.3 collective-permute-start.1
  155.5 2.0 collective-permute-done
  157.4 2.4 copy.126
  159.9 11.5 %collective-permute-done.1 = f32[5,512,22]{1,2,0:T(8,128)} collective-permute-done((f32[5,512,22]{1,2,0:T(8,128)}, f32[5,512,22]{1,2,0:T(8,128)}, u32[]{:S(2)}, u32[]{:S(2)}) %collective-permute-start.1) | collective-permute-done | bytes 225312 | tf_op jit(solution)/shard_map/ppermute | solution.py:52
  171.4 2.4 copy.127
  173.8 12.6 %pad_maximum_fusion = f32[5,512,556]{2,1,0:T(8,128)S(1)} fusion(f32[5,512,22]{2,1,0:T(8,128)} %copy.127, f32[5,128,128]{2,1,0:T(8,128)} %bitcast.254, f32[5,128,128]{2,1,0:T(8,128)} %bitcast.260, f32[5,128,128]{2,1,0:T(8,128)} %bitcast.248, f32[5,128,128]{2,1,0:T(8,128)} %bitcast.242, f32[5,128,128]{2,1,0:T(8,128)} %bitcast.236, ...), kind=kLoop, calls=%fused_computation.74 | loop fusion | flops 24197120 | bytes 11386880 | tf_op jit(solution)/shard_map/concatenate | solution.py:53
  186.6 1.3 collective-permute-start.2
  187.9 1.3 collective-permute-start.3
  190.1 1.3 collective-permute-done.3
  191.6 12.3 %fusion.1 = f32[5,556,276]{1,2,0:T(8,128)S(1)} fusion(f32[5,22,556]{2,1,0:T(8,128)S(1)} %collective-permute-done.3, f32[5,512,22]{2,1,0:T(8,128)S(1)} %copy-done.15, f32[5,128,128]{2,1,0:T(8,128)S(1)} %bitcast.257, f32[5,128,128]{2,1,0:T(8,128)S(1)} %bitcast.263, f32[5,128,128]{2,1,0:T(8,128)S(1)} %bitcast.251, f32[5,128,128]{2,1,0:T(8,128)S(1)} %bitcast.245, ...), kind=kOutput, calls=%fused_computation.34 | convolution fusion | flops 5150962176 | bytes 9252944 | tf_op jit(solution)/shard_map/ih,chw->ciw/dot_general | solution.py:79
  204.0 7.8 %fusion.54 = f32[5,276,276]{2,1,0:T(8,128)S(1)} fusion(f32[5,556,276]{1,2,0:T(8,128)S(1)} %fusion.1, f32[276,276]{1,0:T(8,128)S(1)} %copy-done.16, s32[276]{0:T(512)S(1)} %iota_multiply_fusion.1), kind=kOutput, calls=%fused_computation.90 | convolution fusion | flops 2543913984 | bytes 4898448 | tf_op jit(solution)/shard_map/ciw,jw->cij/dot_general | solution.py:86
  211.8 2.3 convolution_bitcast_fusion
  214.1 1.4 convolution_multiply_fusion
  215.5 1.7 convolution_bitcast_fusion.3
  217.2 1.2 convolution_multiply_fusion.1
  218.5 1.2 collective-permute-start.4
  219.7 3.4 %collective-permute-start.5 = (f32[1,5,64,64]{3,2,1,0:T(8,128)S(1)}, f32[1,5,64,64]{3,2,1,0:T(8,128)S(1)}, u32[]{:S(2)}, u32[]{:S(2)}) collective-permute-start(f32[1,5,64,64]{3,2,1,0:T(8,128)S(1)} %slice_bitcast_fusion), channel_id=1, source_target_pairs={{0,15},{1,0},{2,1},{3,2},{4,3},{5,4},{6,5},{7,6},{8,7},{9,8},{10,9... | collective-permute-start | bytes 245768 | tf_op jit(solution)/shard_map/ppermute | solution.py:33
  224.1 1.3 fusion.66
  225.4 1.6 convolution_bitcast_fusion.1
  227.0 3.0 fusion.64
  229.9 4.5 %fusion.57 = f32[4,258,512]{2,1,0:T(8,128)S(1)} fusion(f32[5,276,276]{2,1,0:T(8,128)S(1)} %fusion.54, f32[258,258]{1,0:T(8,128)S(1)} %fusion.108, s32[258]{0:T(512)S(1)} %iota_multiply_fusion), kind=kOutput, calls=%fused_computation.92 | convolution fusion | flops 1638124544 | bytes 4143104 | tf_op jit(solution)/shard_map/ih,chw->ciw/dot_general | solution.py:79
  234.5 8.8 %fusion.42 = bf16[4,512,512]{2,1,0:T(8,128)(2,1)} fusion(f32[5,512,512]{2,1,0:T(8,128)S(1)} %maximum_maximum_fusion, f32[512,512]{1,0:T(8,128)S(1)} %fusion.67, f32[4,258,512]{2,1,0:T(8,128)S(1)} %fusion.57, s32[258]{0:T(512)S(1)} %iota_multiply_fusion), kind=kOutput, calls=%fused_computation.78 | convolution fusion | flops 3251518464 | bytes 9454600 | tf_op jit(solution)/shard_map/ciw,jw->cij/dot_general | solution.py:86
  243.8 4.4 %collective-permute-start.7 = (f32[1,5,64,64]{3,2,1,0:T(8,128)S(1)}, f32[1,5,64,64]{3,2,1,0:T(8,128)S(1)}, u32[]{:S(2)}, u32[]{:S(2)}) collective-permute-start(f32[1,5,64,64]{3,2,1,0:T(8,128)S(1)} %collective-permute-done.5), channel_id=1, source_target_pairs={{0,15},{1,0},{2,1},{3,2},{4,3},{5,4},{6,5},{7,6},{8,7},{9,8},{10,9... | collective-permute-start | bytes 245768 | tf_op jit(solution)/shard_map/ppermute | solution.py:33
  248.3 3.1 collective-permute-done.6
  251.4 4.4 %collective-permute-start.9 = (f32[1,5,64,64]{3,2,1,0:T(8,128)S(1)}, f32[1,5,64,64]{3,2,1,0:T(8,128)S(1)}, u32[]{:S(2)}, u32[]{:S(2)}) collective-permute-start(f32[1,5,64,64]{3,2,1,0:T(8,128)S(1)} %collective-permute-done.7), channel_id=1, source_target_pairs={{0,15},{1,0},{2,1},{3,2},{4,3},{5,4},{6,5},{7,6},{8,7},{9,8},{10,9... | collective-permute-start | bytes 245768 | tf_op jit(solution)/shard_map/ppermute | solution.py:33
  255.9 2.9 collective-permute-done.8
  258.8 4.5 %collective-permute-start.11 = (f32[1,5,64,64]{3,2,1,0:T(8,128)S(1)}, f32[1,5,64,64]{3,2,1,0:T(8,128)S(1)}, u32[]{:S(2)}, u32[]{:S(2)}) collective-permute-start(f32[1,5,64,64]{3,2,1,0:T(8,128)S(1)} %collective-permute-done.9), channel_id=1, source_target_pairs={{0,15},{1,0},{2,1},{3,2},{4,3},{5,4},{6,5},{7,6},{8,7},{9,8},{10,9... | collective-permute-start | bytes 245768 | tf_op jit(solution)/shard_map/ppermute | solution.py:33
  263.4 3.0 collective-permute-done.10
  266.4 4.4 %collective-permute-start.13 = (f32[1,5,64,64]{3,2,1,0:T(8,128)S(1)}, f32[1,5,64,64]{3,2,1,0:T(8,128)S(1)}, u32[]{:S(2)}, u32[]{:S(2)}) collective-permute-start(f32[1,5,64,64]{3,2,1,0:T(8,128)S(1)} %collective-permute-done.11), channel_id=1, source_target_pairs={{0,15},{1,0},{2,1},{3,2},{4,3},{5,4},{6,5},{7,6},{8,7},{9,8},{10,9... | collective-permute-start | bytes 245768 | tf_op jit(solution)/shard_map/ppermute | solution.py:33
  270.9 3.1 collective-permute-done.12
  273.9 4.4 %collective-permute-start.15 = (f32[1,5,64,64]{3,2,1,0:T(8,128)S(1)}, f32[1,5,64,64]{3,2,1,0:T(8,128)S(1)}, u32[]{:S(2)}, u32[]{:S(2)}) collective-permute-start(f32[1,5,64,64]{3,2,1,0:T(8,128)S(1)} %collective-permute-done.13), channel_id=1, source_target_pairs={{0,15},{1,0},{2,1},{3,2},{4,3},{5,4},{6,5},{7,6},{8,7},{9,8},{10,9... | collective-permute-start | bytes 245768 | tf_op jit(solution)/shard_map/ppermute | solution.py:33
  278.4 3.1 collective-permute-done.14
  281.5 4.4 %collective-permute-start.17 = (f32[1,5,64,64]{3,2,1,0:T(8,128)S(1)}, f32[1,5,64,64]{3,2,1,0:T(8,128)S(1)}, u32[]{:S(2)}, u32[]{:S(2)}) collective-permute-start(f32[1,5,64,64]{3,2,1,0:T(8,128)S(1)} %collective-permute-done.15), channel_id=1, source_target_pairs={{0,15},{1,0},{2,1},{3,2},{4,3},{5,4},{6,5},{7,6},{8,7},{9,8},{10,9... | collective-permute-start | bytes 245768 | tf_op jit(solution)/shard_map/ppermute | solution.py:33
  285.9 2.9 collective-permute-done.16
  289.2 7.4 %collective-permute-done.18 = f32[1,5,64,64]{3,2,1,0:T(8,128)S(1)} collective-permute-done((f32[1,5,64,64]{3,2,1,0:T(8,128)S(1)}, f32[1,5,64,64]{3,2,1,0:T(8,128)S(1)}, u32[]{:S(2)}, u32[]{:S(2)}) %collective-permute-start.18) | collective-permute-done | bytes 81952 | tf_op jit(solution)/shard_map/ppermute | solution.py:28
  296.5 1.6 copy.134
  298.2 1.5 slice.255
  299.7 1.7 reshape.369
  301.4 3.0 fusion.61
  304.4 1.2 fusion.86
  305.6 0.7 fusion.363
  306.3 2.2 convolution_bitcast_fusion.2
  308.5 1.2 copy.132
  309.7 1.5 slice.198
  311.6 4.4 %fusion.65 = bf16[4,128,512]{2,1,0:T(8,128)(2,1)} fusion(f32[4,128,258]{1,2,0:T(8,128)} %convolution_bitcast_fusion.2, f32[4,128,512]{2,1,0:T(8,128)} %slice.198, f32[128,512]{1,0:T(8,128)S(1)} %max.70, s32[258]{0:T(512)S(1)} %iota_multiply_fusion), kind=kOutput, calls=%fused_computation.101 | convolution fusion | flops 814365696 | bytes 2364424 | tf_op jit(solution)/shard_map/ciw,jw->cij/dot_general | solution.py:86
  (115 shorter events, 8.8 us)
Async XLA Ops:
  6.8 21.2 %all-to-all-start = ((bf16[16,2,5]{2,1,0:T(2,128)(2,1)}), bf16[16,2,5]{2,1,0:T(2,128)(2,1)S(1)}, u32[]{:S(2)}, u32[]{:S(2)}) async-start(bf16[16,2,5]{2,1,0:T(2,128)(2,1)} %broadcast_select_fusion.1), calls=%async_computation | async-start | bytes 16384 | tf_op jit(solution)/shard_map/all_to_all | solution.py:153
  28.0 84.2 %all-to-all-start.1 = ((bf16[32,4,16384]{2,1,0:T(4,128)(2,1)}), bf16[32,4,16384]{2,1,0:T(4,128)(2,1)}, u32[]{:S(2)}, u32[]{:S(2)}) async-start(bf16[32,4,16384]{2,1,0:T(4,128)(2,1)} %broadcast_select_fusion), calls=%async_computation.1 | async-start | bytes 8388608 | tf_op jit(solution)/shard_map/all_to_all | solution.py:152
  121.2 10.9 %copy-start.12 = (f32[16,1,128,128]{3,0,2,1:T(8,128)S(1)}, f32[16,1,128,128]{3,0,2,1:T(8,128)}, u32[]{:S(2)}) copy-start(f32[16,1,128,128]{3,0,2,1:T(8,128)} %fusion.58) | copy-start | bytes 3145732
  137.6 1.7 copy-start
  137.6 1.7 copy-start.2
  137.6 1.7 copy-start.4
  137.6 1.7 copy-start.6
  137.6 1.7 copy-start.8
  137.6 1.7 copy-start.10
  142.9 14.5 %collective-permute-start = (f32[5,512,22]{1,2,0:T(8,128)}, f32[5,512,22]{1,2,0:T(8,128)}, u32[]{:S(2)}, u32[]{:S(2)}) collective-permute-start(f32[5,512,22]{1,2,0:T(8,128)} %copy.124), channel_id=1, source_target_pairs={{0,2},{2,4},{4,6},{6,8},{8,10},{10,12},{12,14},{1,3},{3,5},{5,7},{... | collective-permute-start | bytes 675848 | tf_op jit(solution)/shard_map/ppermute | solution.py:49
  154.1 17.3 %collective-permute-start.1 = (f32[5,512,22]{1,2,0:T(8,128)}, f32[5,512,22]{1,2,0:T(8,128)}, u32[]{:S(2)}, u32[]{:S(2)}) collective-permute-start(f32[5,512,22]{1,2,0:T(8,128)} %copy.125), channel_id=1, source_target_pairs={{2,0},{4,2},{6,4},{8,6},{10,8},{12,10},{14,12},{3,1},{5,3},{7,5},{... | collective-permute-start | bytes 675848 | tf_op jit(solution)/shard_map/ppermute | solution.py:52
  173.8 15.4 %copy-start.1 = (f32[1,5,128,128]{3,0,2,1:T(1,128)S(1)}, f32[1,5,128,128]{3,0,2,1:T(1,128)}, u32[]{:S(2)}) copy-start(f32[1,5,128,128]{3,0,2,1:T(1,128)} %copy-done) | copy-start | bytes 983044
  173.8 15.4 %copy-start.3 = (f32[1,5,128,128]{3,0,2,1:T(1,128)S(1)}, f32[1,5,128,128]{3,0,2,1:T(1,128)}, u32[]{:S(2)}) copy-start(f32[1,5,128,128]{3,0,2,1:T(1,128)} %copy-done.2) | copy-start | bytes 983044
  173.8 15.4 %copy-start.5 = (f32[1,5,128,128]{3,0,2,1:T(1,128)S(1)}, f32[1,5,128,128]{3,0,2,1:T(1,128)}, u32[]{:S(2)}) copy-start(f32[1,5,128,128]{3,0,2,1:T(1,128)} %copy-done.4) | copy-start | bytes 983044
  173.8 15.4 %copy-start.7 = (f32[1,5,128,128]{3,0,2,1:T(1,128)S(1)}, f32[1,5,128,128]{3,0,2,1:T(1,128)}, u32[]{:S(2)}) copy-start(f32[1,5,128,128]{3,0,2,1:T(1,128)} %copy-done.6) | copy-start | bytes 983044
  173.8 15.4 %copy-start.9 = (f32[1,5,128,128]{3,0,2,1:T(1,128)S(1)}, f32[1,5,128,128]{3,0,2,1:T(1,128)}, u32[]{:S(2)}) copy-start(f32[1,5,128,128]{3,0,2,1:T(1,128)} %copy-done.8) | copy-start | bytes 983044
  173.8 15.4 %copy-start.11 = (f32[1,5,128,128]{3,0,2,1:T(1,128)S(1)}, f32[1,5,128,128]{3,0,2,1:T(1,128)}, u32[]{:S(2)}) copy-start(f32[1,5,128,128]{3,0,2,1:T(1,128)} %copy-done.10) | copy-start | bytes 983044
  186.6 3.5 %collective-permute-start.2 = (f32[5,22,556]{2,1,0:T(8,128)S(1)}, f32[5,22,556]{2,1,0:T(8,128)S(1)}, u32[]{:S(2)}, u32[]{:S(2)}) collective-permute-start(f32[5,22,556]{2,1,0:T(8,128)S(1)} %get-tuple-element.11), channel_id=1, source_target_pairs={{0,1},{2,3},{4,5},{6,7},{8,9},{10,11},{12,13},{14,15},{16,17},{18,... | collective-permute-start | bytes 733928 | tf_op jit(solution)/shard_map/ppermute | solution.py:49
  187.9 3.5 %collective-permute-start.3 = (f32[5,22,556]{2,1,0:T(8,128)S(1)}, f32[5,22,556]{2,1,0:T(8,128)S(1)}, u32[]{:S(2)}, u32[]{:S(2)}) collective-permute-start(f32[5,22,556]{2,1,0:T(8,128)S(1)} %get-tuple-element.12), channel_id=1, source_target_pairs={{1,0},{3,2},{5,4},{7,6},{9,8},{11,10},{13,12},{15,14},{17,16},{19,... | collective-permute-start | bytes 733928 | tf_op jit(solution)/shard_map/ppermute | solution.py:52
  189.9 1.5 copy-start.14
  189.9 1.7 copy-start.15
  190.0 13.9 %copy-start.16 = (f32[276,276]{1,0:T(8,128)S(1)}, f32[276,276]{1,0:T(8,128)}, u32[]{:S(2)}) copy-start(f32[276,276]{1,0:T(8,128)} %and_convert_fusion) | copy-start | bytes 914116
  218.5 25.2 %collective-permute-start.4 = (f32[1,5,64,64]{3,2,1,0:T(8,128)S(1)}, f32[1,5,64,64]{3,2,1,0:T(8,128)S(1)}, u32[]{:S(2)}, u32[]{:S(2)}) collective-permute-start(f32[1,5,64,64]{3,2,1,0:T(8,128)S(1)} %slice_bitcast_fusion), channel_id=1, source_target_pairs={{0,1},{1,2},{2,3},{3,4},{4,5},{5,6},{6,7},{7,8},{8,9},{9,10},{10,1... | collective-permute-start | bytes 245768 | tf_op jit(solution)/shard_map/ppermute | solution.py:28
  219.7 24.1 %collective-permute-start.5 = (f32[1,5,64,64]{3,2,1,0:T(8,128)S(1)}, f32[1,5,64,64]{3,2,1,0:T(8,128)S(1)}, u32[]{:S(2)}, u32[]{:S(2)}) collective-permute-start(f32[1,5,64,64]{3,2,1,0:T(8,128)S(1)} %slice_bitcast_fusion), channel_id=1, source_target_pairs={{0,15},{1,0},{2,1},{3,2},{4,3},{5,4},{6,5},{7,6},{8,7},{9,8},{10,9... | collective-permute-start | bytes 245768 | tf_op jit(solution)/shard_map/ppermute | solution.py:33
  243.8 7.6 %collective-permute-start.6 = (f32[1,5,64,64]{3,2,1,0:T(8,128)S(1)}, f32[1,5,64,64]{3,2,1,0:T(8,128)S(1)}, u32[]{:S(2)}, u32[]{:S(2)}) collective-permute-start(f32[1,5,64,64]{3,2,1,0:T(8,128)S(1)} %collective-permute-done.4), channel_id=1, source_target_pairs={{0,1},{1,2},{2,3},{3,4},{4,5},{5,6},{6,7},{7,8},{8,9},{9,10},{10,1... | collective-permute-start | bytes 245768 | tf_op jit(solution)/shard_map/ppermute | solution.py:28
  243.8 7.5 %collective-permute-start.7 = (f32[1,5,64,64]{3,2,1,0:T(8,128)S(1)}, f32[1,5,64,64]{3,2,1,0:T(8,128)S(1)}, u32[]{:S(2)}, u32[]{:S(2)}) collective-permute-start(f32[1,5,64,64]{3,2,1,0:T(8,128)S(1)} %collective-permute-done.5), channel_id=1, source_target_pairs={{0,15},{1,0},{2,1},{3,2},{4,3},{5,4},{6,5},{7,6},{8,7},{9,8},{10,9... | collective-permute-start | bytes 245768 | tf_op jit(solution)/shard_map/ppermute | solution.py:33
  251.4 7.4 %collective-permute-start.8 = (f32[1,5,64,64]{3,2,1,0:T(8,128)S(1)}, f32[1,5,64,64]{3,2,1,0:T(8,128)S(1)}, u32[]{:S(2)}, u32[]{:S(2)}) collective-permute-start(f32[1,5,64,64]{3,2,1,0:T(8,128)S(1)} %collective-permute-done.6), channel_id=1, source_target_pairs={{0,1},{1,2},{2,3},{3,4},{4,5},{5,6},{6,7},{7,8},{8,9},{9,10},{10,1... | collective-permute-start | bytes 245768 | tf_op jit(solution)/shard_map/ppermute | solution.py:28
  251.4 7.4 %collective-permute-start.9 = (f32[1,5,64,64]{3,2,1,0:T(8,128)S(1)}, f32[1,5,64,64]{3,2,1,0:T(8,128)S(1)}, u32[]{:S(2)}, u32[]{:S(2)}) collective-permute-start(f32[1,5,64,64]{3,2,1,0:T(8,128)S(1)} %collective-permute-done.7), channel_id=1, source_target_pairs={{0,15},{1,0},{2,1},{3,2},{4,3},{5,4},{6,5},{7,6},{8,7},{9,8},{10,9... | collective-permute-start | bytes 245768 | tf_op jit(solution)/shard_map/ppermute | solution.py:33
  258.8 7.5 %collective-permute-start.10 = (f32[1,5,64,64]{3,2,1,0:T(8,128)S(1)}, f32[1,5,64,64]{3,2,1,0:T(8,128)S(1)}, u32[]{:S(2)}, u32[]{:S(2)}) collective-permute-start(f32[1,5,64,64]{3,2,1,0:T(8,128)S(1)} %collective-permute-done.8), channel_id=1, source_target_pairs={{0,1},{1,2},{2,3},{3,4},{4,5},{5,6},{6,7},{7,8},{8,9},{9,10},{10,1... | collective-permute-start | bytes 245768 | tf_op jit(solution)/shard_map/ppermute | solution.py:28
  258.8 7.5 %collective-permute-start.11 = (f32[1,5,64,64]{3,2,1,0:T(8,128)S(1)}, f32[1,5,64,64]{3,2,1,0:T(8,128)S(1)}, u32[]{:S(2)}, u32[]{:S(2)}) collective-permute-start(f32[1,5,64,64]{3,2,1,0:T(8,128)S(1)} %collective-permute-done.9), channel_id=1, source_target_pairs={{0,15},{1,0},{2,1},{3,2},{4,3},{5,4},{6,5},{7,6},{8,7},{9,8},{10,9... | collective-permute-start | bytes 245768 | tf_op jit(solution)/shard_map/ppermute | solution.py:33
  266.4 7.5 %collective-permute-start.12 = (f32[1,5,64,64]{3,2,1,0:T(8,128)S(1)}, f32[1,5,64,64]{3,2,1,0:T(8,128)S(1)}, u32[]{:S(2)}, u32[]{:S(2)}) collective-permute-start(f32[1,5,64,64]{3,2,1,0:T(8,128)S(1)} %collective-permute-done.10), channel_id=1, source_target_pairs={{0,1},{1,2},{2,3},{3,4},{4,5},{5,6},{6,7},{7,8},{8,9},{9,10},{10,1... | collective-permute-start | bytes 245768 | tf_op jit(solution)/shard_map/ppermute | solution.py:28
  266.4 7.5 %collective-permute-start.13 = (f32[1,5,64,64]{3,2,1,0:T(8,128)S(1)}, f32[1,5,64,64]{3,2,1,0:T(8,128)S(1)}, u32[]{:S(2)}, u32[]{:S(2)}) collective-permute-start(f32[1,5,64,64]{3,2,1,0:T(8,128)S(1)} %collective-permute-done.11), channel_id=1, source_target_pairs={{0,15},{1,0},{2,1},{3,2},{4,3},{5,4},{6,5},{7,6},{8,7},{9,8},{10,9... | collective-permute-start | bytes 245768 | tf_op jit(solution)/shard_map/ppermute | solution.py:33
  273.9 7.5 %collective-permute-start.14 = (f32[1,5,64,64]{3,2,1,0:T(8,128)S(1)}, f32[1,5,64,64]{3,2,1,0:T(8,128)S(1)}, u32[]{:S(2)}, u32[]{:S(2)}) collective-permute-start(f32[1,5,64,64]{3,2,1,0:T(8,128)S(1)} %collective-permute-done.12), channel_id=1, source_target_pairs={{0,1},{1,2},{2,3},{3,4},{4,5},{5,6},{6,7},{7,8},{8,9},{9,10},{10,1... | collective-permute-start | bytes 245768 | tf_op jit(solution)/shard_map/ppermute | solution.py:28
  273.9 7.5 %collective-permute-start.15 = (f32[1,5,64,64]{3,2,1,0:T(8,128)S(1)}, f32[1,5,64,64]{3,2,1,0:T(8,128)S(1)}, u32[]{:S(2)}, u32[]{:S(2)}) collective-permute-start(f32[1,5,64,64]{3,2,1,0:T(8,128)S(1)} %collective-permute-done.13), channel_id=1, source_target_pairs={{0,15},{1,0},{2,1},{3,2},{4,3},{5,4},{6,5},{7,6},{8,7},{9,8},{10,9... | collective-permute-start | bytes 245768 | tf_op jit(solution)/shard_map/ppermute | solution.py:33
  281.5 7.4 %collective-permute-start.16 = (f32[1,5,64,64]{3,2,1,0:T(8,128)S(1)}, f32[1,5,64,64]{3,2,1,0:T(8,128)S(1)}, u32[]{:S(2)}, u32[]{:S(2)}) collective-permute-start(f32[1,5,64,64]{3,2,1,0:T(8,128)S(1)} %collective-permute-done.14), channel_id=1, source_target_pairs={{0,1},{1,2},{2,3},{3,4},{4,5},{5,6},{6,7},{7,8},{8,9},{9,10},{10,1... | collective-permute-start | bytes 245768 | tf_op jit(solution)/shard_map/ppermute | solution.py:28
  281.5 7.7 %collective-permute-start.17 = (f32[1,5,64,64]{3,2,1,0:T(8,128)S(1)}, f32[1,5,64,64]{3,2,1,0:T(8,128)S(1)}, u32[]{:S(2)}, u32[]{:S(2)}) collective-permute-start(f32[1,5,64,64]{3,2,1,0:T(8,128)S(1)} %collective-permute-done.15), channel_id=1, source_target_pairs={{0,15},{1,0},{2,1},{3,2},{4,3},{5,4},{6,5},{7,6},{8,7},{9,8},{10,9... | collective-permute-start | bytes 245768 | tf_op jit(solution)/shard_map/ppermute | solution.py:33
  288.9 7.6 %collective-permute-start.18 = (f32[1,5,64,64]{3,2,1,0:T(8,128)S(1)}, f32[1,5,64,64]{3,2,1,0:T(8,128)S(1)}, u32[]{:S(2)}, u32[]{:S(2)}) collective-permute-start(f32[1,5,64,64]{3,2,1,0:T(8,128)S(1)} %collective-permute-done.16), channel_id=1, source_target_pairs={{0,1},{1,2},{2,3},{3,4},{4,5},{5,6},{6,7},{7,8},{8,9},{9,10},{10,1... | collective-permute-start | bytes 245768 | tf_op jit(solution)/shard_map/ppermute | solution.py:28
  301.4 7.1 %copy-start.13 = (f32[4,2,64,8,64]{4,2,0,1,3:T(8,128)S(1)}, f32[4,2,64,8,64]{4,2,0,1,3:T(8,128)}, u32[]{:S(2)}) copy-start(f32[4,2,64,8,64]{4,2,0,1,3:T(8,128)} %slice.255) | copy-start | bytes 3145732
